TPU v7x, 512 devices: a whole 4x8x8 slice. The times are simulated.
512 devices in a mesh: section: 8 (over y), expert: 32 (over z, x_hi, core), dp: 2 (over x_lo).
Axes of the slice: x: 4 (x_hi: 2, x_lo: 2; x = x_hi * 2 + x_lo), y: 8, z: 8, core: 2. Of those that a mesh axis runs over, the one named last changes fastest.
Arguments:
- blocks: bfloat16 [8, 512, 7168], P('section', ('expert', 'dp')), may hold values from -6 to 6
- gains: float32 [8, 7168], P('section'), may hold values from 0.1 to 1.9
- w_gate: bfloat16 [8, 7168, 4096], P('section', 'dp', 'expert'), may hold values from -0.0625 to 0.0625
- w_up: bfloat16 [8, 7168, 4096], P('section', 'dp', 'expert'), may hold values from -0.0625 to 0.0625
- w_down: bfloat16 [8, 7168, 4096], P('section', 'dp', 'expert'), may hold values from -0.1875 to 0.1875
- expert_ids: int32 [8, 2, 512, 2], P('section', None, ('expert', 'dp')), may hold values from 0 to 3, all different within a row; in each aligned block of 8 rows (0 to 7, 8 to 15, ..., all dimensions but the last counted through in order) at most 5 rows name the same one
- combine: float32 [8, 2, 512, 2], P('section', None, ('expert', 'dp')), may hold values from 0.2 to 1
Outputs:
- finished: bfloat16 [8, 512, 7168], P('section', ('expert', 'dp'))
Inputs may be any that keep to these rules, and one draw needn't show every extreme that they name: `expert_ids`: each token names 2 different experts; within the 8 tokens of one device (aligned blocks), no expert is named more than 5 times, a bound that some block reaches.
All inputs are finite; a program needn't handle non-finite values.
Results may differ from a plain program's by a relative error of at most 0.0073.
Values may be sent and summed in bfloat16 or wider, within the bound.
No kernel may reach another device: no remote copies, remote signals or barrier semaphores. Data moves between devices by JAX's collectives and lax.ppermute only.
A program may use at most 64 MiB of HBM per device.

v0:
```python
from functools import partial
import jax
import jax.numpy as jnp
import numpy as np
from jax import lax
from jax.sharding import Mesh
from jax.sharding import PartitionSpec as P

ALL = ("eg", "q", "dp")


def passed_along(array, axis, by):
    length = lax.axis_size(axis)
    return lax.ppermute(array, axis, [(i, (i + by) % length) for i in range(length)])


def route(stream, gain_row, routes, experts, capacity):
    tok_rows, model_width = stream.shape
    fan_out = routes.shape[1]
    widened = stream.astype(jnp.float32)
    inv_rms = lax.rsqrt(jnp.mean(widened * widened, axis=1, keepdims=True) + 1e-06)
    normed = (widened * inv_rms * gain_row[None, :]).astype(jnp.bfloat16)
    flat_ids = routes.reshape(-1)
    count_all = flat_ids.shape[0]
    chosen = (flat_ids[:, None] == jnp.arange(experts, dtype=jnp.int32)[None, :]).astype(
        jnp.float32
    )
    triangle = (jnp.arange(count_all)[:, None] >= jnp.arange(count_all)[None, :]).astype(
        jnp.float32
    )
    running = jnp.dot(triangle, chosen, preferred_element_type=jnp.float32)
    slot_of = jnp.sum(chosen * (running - 1.0), axis=1).astype(jnp.int32)
    target = flat_ids * capacity + slot_of
    placing = jnp.arange(experts * capacity, dtype=jnp.int32)[:, None] == target[None, :]
    placing = (
        placing.reshape(experts * capacity, tok_rows, fan_out).any(axis=2).astype(jnp.bfloat16)
    )
    outgoing = jnp.dot(placing, normed, preferred_element_type=jnp.float32).astype(jnp.bfloat16)
    return (widened, outgoing.reshape(experts, capacity, model_width), target)


def moe_layer(stream, gain_row, gate_w, up_w, down_mine, routes, mixing):
    experts = lax.axis_size("eg")
    blocks = lax.axis_size("q")
    halves = lax.axis_size("dp")
    tok_rows, model_width = stream.shape
    fan_out = routes.shape[1]
    capacity = min(tok_rows, max(2, 5 * tok_rows * fan_out // (4 * experts)))
    half = model_width // halves
    widened, outgoing, target = route(stream, gain_row, routes, experts, capacity)
    send = outgoing.reshape(experts, 1, capacity, halves, half).transpose(0, 1, 3, 2, 4)
    send = jnp.broadcast_to(send, (experts, blocks, halves, capacity, half))
    send = send.reshape(experts * blocks * halves, capacity, half)
    arrived = lax.all_to_all(send, ALL, split_axis=0, concat_axis=0, tiled=True)
    sources = arrived.shape[0]
    rows = arrived.reshape(sources * capacity, half)
    gate_part = jnp.dot(rows, gate_w, preferred_element_type=jnp.float32)
    up_part = jnp.dot(rows, up_w, preferred_element_type=jnp.float32)
    both = lax.psum(jnp.stack([gate_part, up_part]), "dp")
    hidden = (jax.nn.silu(both[0]) * both[1]).astype(jnp.bfloat16)
    hidden_all = lax.all_gather(hidden, "q", axis=1, tiled=True)
    out = lax.dot_general(
        hidden_all, down_mine, (((1,), (1,)), ((), ())), preferred_element_type=jnp.float32
    ).astype(jnp.bfloat16)
    piece = out.shape[1]
    back = lax.all_to_all(
        out.reshape(sources, capacity, piece), ALL, split_axis=0, concat_axis=0, tiled=True
    )
    back = back.reshape(experts, blocks, halves, capacity, piece).transpose(0, 3, 2, 1, 4)
    expert_out = back.reshape(experts * capacity, model_width)
    picked = jnp.take(expert_out, target, axis=0)
    picked = picked.reshape(tok_rows, fan_out, model_width)
    mixed_sum = jnp.sum(mixing[:, :, None] * picked.astype(jnp.float32), axis=1)
    return (widened + mixed_sum).astype(jnp.bfloat16)


def on_device(blocks, gains, w_gate, w_up, w_down, expert_ids, combine):
    stream = blocks[0]
    turns = expert_ids.shape[1]
    n_blocks = lax.axis_size("q")
    down_local = w_down[0]
    half, width = down_local.shape
    piece = half // n_blocks
    down_mine = lax.all_to_all(
        down_local.reshape(n_blocks, piece, width), "q", split_axis=0, concat_axis=0, tiled=True
    )
    down_mine = down_mine.transpose(1, 0, 2).reshape(piece, n_blocks * width)
    for layer_turn in range(turns):
        if layer_turn > 0:
            stream = passed_along(stream, "section", 1)
        stream = moe_layer(
            stream,
            gains[0],
            w_gate[0],
            w_up[0],
            down_mine,
            expert_ids[0, layer_turn],
            combine[0, layer_turn],
        )
    return stream[None]


def solution(mesh):
    n_section, n_expert, n_dp = (mesh.shape[a] for a in ("section", "expert", "dp"))
    n_q = n_expert // 4
    inner = Mesh(
        np.asarray(mesh.devices).reshape(n_section, n_expert // n_q, n_q, n_dp),
        ("section", "eg", "q", "dp"),
    )
    tok = ("eg", "q", "dp")
    in_specs = (
        P("section", tok, None),
        P("section", None),
        P("section", "dp", ("eg", "q")),
        P("section", "dp", ("eg", "q")),
        P("section", "dp", ("eg", "q")),
        P("section", None, tok, None),
        P("section", None, tok, None),
    )
    out_specs = P("section", tok, None)
    return jax.shard_map(
        on_device, mesh=inner, in_specs=in_specs, out_specs=out_specs, check_vma=False
    )
```

profile of v0, /device:TPU:1, one launch (start us, length us, event | category | flops | bytes accessed | tf_op | source)
XLA Modules:
  0.0 413.9 jit_solution(5506339195129914146)
XLA Ops:
  6.5 0.8 fusion.36
  9.1 1.1 fusion.16
  10.2 1.2 convolution_convert_fusion.1
  12.0 98.3 %all_to_all.25 = bf16[64,5,3584]{2,1,0:T(8,128)(2,1)} all-to-all(bf16[64,5,3584]{2,1,0:T(8,128)(2,1)S(1)} %bitcast.103), channel_id=1, replica_groups=mesh['section'=8,'eg'=4,'q'=8,'dp'=2] {'eg','q','dp'}, dimensions={0} | all-to-all | bytes 4587520 | tf_op jit(solution)/shard_map/all_to_all | solution.py:54
  110.3 6.3 %all-to-all-start.1 = ((bf16[8,448,128]{2,1,0:T(8,128)(2,1)}), bf16[8,448,128]{2,1,0:T(8,128)(2,1)}, u32[]{:S(2)}, u32[]{:S(2)}) async-start(bf16[8,448,128]{2,1,0:T(8,128)(2,1)} %bitcast.14), calls=%async_computation.1 | async-start | bytes 1835008 | tf_op jit(solution)/shard_map/all_to_all | solution.py:84
  116.6 3.2 reshape.111
  122.5 39.6 %all-reduce.3.cloned.1.call-done = f32[2,320,128]{2,1,0:T(8,128)} async-done(((f32[2,320,128]{2,1,0:T(8,128)}), f32[2,320,128]{2,1,0:T(8,128)}) %all-reduce.3.cloned.1.call-update) | async-done | bytes 327696 | tf_op jit(solution)/shard_map/psum | solution.py:59
  162.1 1.1 fusion.23
  163.2 17.1 %all_gather.6 = bf16[320,1024]{1,0:T(8,128)(2,1)S(1)} all-gather(bf16[320,128]{1,0:T(8,128)(2,1)S(1)} %fusion.23), channel_id=1, replica_groups=mesh['section'=8,'eg'=4,'q'=8,'dp'=2] {'q'}, dimensions={1}, use_global_device_ids=true | all-gather | bytes 737280 | tf_op jit(solution)/shard_map/all_gather | solution.py:61
  180.3 1.7 convolution_convert_fusion.3
  182.0 1.0 reshape.113
  182.9 9.5 %all-to-all-start.2 = ((bf16[64,5,448]{2,1,0:T(8,128)(2,1)}), bf16[64,5,448]{2,1,0:T(8,128)(2,1)S(1)}, u32[]{:S(2)}, u32[]{:S(2)}) async-start(bf16[64,5,448]{2,1,0:T(8,128)(2,1)} %reshape.113), calls=%async_computation.2 | async-start | bytes 1048576 | tf_op jit(solution)/shard_map/all_to_all | solution.py:66
  192.6 18.0 %all-to-all-done.2 = bf16[64,5,448]{2,1,0:T(8,128)(2,1)S(1)} async-done(((bf16[64,5,448]{2,1,0:T(8,128)(2,1)}), bf16[64,5,448]{2,1,0:T(8,128)(2,1)S(1)}, u32[]{:S(2)}, u32[]{:S(2)}) %all-to-all-start.2) | async-done | bytes 286752 | tf_op jit(solution)/shard_map/all_to_all | solution.py:66
  213.0 3.1 collective-permute-start
  216.2 4.2 %collective-permute-done = bf16[8,7168]{1,0:T(8,128)(2,1)S(1)} collective-permute-done((bf16[8,7168]{1,0:T(8,128)(2,1)S(1)}, bf16[8,7168]{1,0:T(8,128)(2,1)S(1)}, u32[]{:S(2)}, u32[]{:S(2)}) %collective-permute-start) | collective-permute-done | bytes 114720 | tf_op jit(solution)/shard_map/ppermute | solution.py:14
  221.6 89.4 %all_to_all.26 = bf16[64,5,3584]{2,1,0:T(8,128)(2,1)} all-to-all(bf16[64,5,3584]{2,1,0:T(8,128)(2,1)S(1)} %bitcast.104), channel_id=1, replica_groups=mesh['section'=8,'eg'=4,'q'=8,'dp'=2] {'eg','q','dp'}, dimensions={0} | all-to-all | bytes 4587520 | tf_op jit(solution)/shard_map/all_to_all | solution.py:54
  310.9 3.2 reshape.117
  316.8 38.8 %all-reduce.5.cloned.1.call-done = f32[2,320,128]{2,1,0:T(8,128)} async-done(((f32[2,320,128]{2,1,0:T(8,128)}), f32[2,320,128]{2,1,0:T(8,128)}) %all-reduce.5.cloned.1.call-update) | async-done | bytes 327696 | tf_op jit(solution)/shard_map/psum | solution.py:59
  355.6 1.1 fusion.21
  356.7 17.1 %all_gather.7 = bf16[320,1024]{1,0:T(8,128)(2,1)S(1)} all-gather(bf16[320,128]{1,0:T(8,128)(2,1)S(1)} %fusion.21), channel_id=1, replica_groups=mesh['section'=8,'eg'=4,'q'=8,'dp'=2] {'q'}, dimensions={1}, use_global_device_ids=true | all-gather | bytes 737280 | tf_op jit(solution)/shard_map/all_gather | solution.py:61
  373.8 1.7 convolution_convert_fusion.2
  375.5 1.0 reshape.118
  376.5 9.5 %all-to-all-start.4 = ((bf16[64,5,448]{2,1,0:T(8,128)(2,1)}), bf16[64,5,448]{2,1,0:T(8,128)(2,1)S(1)}, u32[]{:S(2)}, u32[]{:S(2)}) async-start(bf16[64,5,448]{2,1,0:T(8,128)(2,1)} %reshape.118), calls=%async_computation.4 | async-start | bytes 1048576 | tf_op jit(solution)/shard_map/all_to_all | solution.py:66
  386.1 18.0 %all-to-all-done.4 = bf16[64,5,448]{2,1,0:T(8,128)(2,1)S(1)} async-done(((bf16[64,5,448]{2,1,0:T(8,128)(2,1)}), bf16[64,5,448]{2,1,0:T(8,128)(2,1)S(1)}, u32[]{:S(2)}, u32[]{:S(2)}) %all-to-all-start.4) | async-done | bytes 286752 | tf_op jit(solution)/shard_map/all_to_all | solution.py:66
  (69 shorter events, 14.4 us)
Async XLA Ops:
  6.5 113.2 %copy-start = (bf16[1,3584,128]{2,1,0:T(8,128)(2,1)S(1)}, bf16[1,3584,128]{2,1,0:T(8,128)(2,1)}, u32[]{:S(2)}) copy-start(bf16[1,3584,128]{2,1,0:T(8,128)(2,1)} %param.12) | copy-start | bytes 2752516
  110.3 70.0 %all-to-all-start.1 = ((bf16[8,448,128]{2,1,0:T(8,128)(2,1)}), bf16[8,448,128]{2,1,0:T(8,128)(2,1)}, u32[]{:S(2)}, u32[]{:S(2)}) async-start(bf16[8,448,128]{2,1,0:T(8,128)(2,1)} %bitcast.14), calls=%async_computation.1 | async-start | bytes 1835008 | tf_op jit(solution)/shard_map/all_to_all | solution.py:84
  116.5 45.6 %all-reduce.3.cloned.1.call-start = ((), (), s32[]{:S(2)}) async-start(), calls=%async_computation.5 | async-start | bytes 655360 | tf_op jit(solution)/shard_map/psum | solution.py:59
  119.8 1.2 copy-start.1
  180.3 12.2 %copy-start.5 = (f32[1,2,8,2]{2,3,1,0:T(2,128)S(1)}, f32[1,2,8,2]{2,3,1,0:T(2,128)}, u32[]{:S(2)}) copy-start(f32[1,2,8,2]{2,3,1,0:T(2,128)} %param.15) | copy-start | bytes 388
  182.9 27.7 %all-to-all-start.2 = ((bf16[64,5,448]{2,1,0:T(8,128)(2,1)}), bf16[64,5,448]{2,1,0:T(8,128)(2,1)S(1)}, u32[]{:S(2)}, u32[]{:S(2)}) async-start(bf16[64,5,448]{2,1,0:T(8,128)(2,1)} %reshape.113), calls=%async_computation.2 | async-start | bytes 1048576 | tf_op jit(solution)/shard_map/all_to_all | solution.py:66
  192.5 163.2 %all-reduce.5.cloned.1.call-start = ((), (), s32[]{:S(2)}) async-start(), calls=%async_computation.6 | async-start | bytes 655360 | tf_op jit(solution)/shard_map/psum | solution.py:59
  211.2 1.7 copy-start.3
  211.2 9.4 %copy-start.4 = (f32[1,7168]{1,0:T(1,128)S(1)}, f32[1,7168]{1,0:T(1,128)}, u32[]{:S(2)}) copy-start(f32[1,7168]{1,0:T(1,128)} %param.10) | copy-start | bytes 86020
  213.0 7.4 %collective-permute-start = (bf16[8,7168]{1,0:T(8,128)(2,1)S(1)}, bf16[8,7168]{1,0:T(8,128)(2,1)S(1)}, u32[]{:S(2)}, u32[]{:S(2)}) collective-permute-start(bf16[8,7168]{1,0:T(8,128)(2,1)S(1)} %fusion.19), channel_id=1, source_target_pairs={{0,64},{64,128},{128,192},{192,256},{256,320},{320,384},{384,448},... | collective-permute-start | bytes 344072 | tf_op jit(solution)/shard_map/ppermute | solution.py:14
  314.1 1.2 copy-start.2
  376.5 27.7 %all-to-all-start.4 = ((bf16[64,5,448]{2,1,0:T(8,128)(2,1)}), bf16[64,5,448]{2,1,0:T(8,128)(2,1)S(1)}, u32[]{:S(2)}, u32[]{:S(2)}) async-start(bf16[64,5,448]{2,1,0:T(8,128)(2,1)} %reshape.118), calls=%async_computation.4 | async-start | bytes 1048576 | tf_op jit(solution)/shard_map/all_to_all | solution.py:66
Sparse Core Ops, SparseCore 0:
  122.6 39.4 all-reduce.2
  316.9 38.6 all-reduce.4
where the time goes:
time: 415 us; the launch traced here: 414 us
  blocking collectives  222 us (53%)
  waiting for transfers between devices  119 us (29%)
  starting transfers between devices  28.4 us (7%)
  local copies, waits for them, and re-layouts  15 us (4%)
  between operations  13.7 us (3%)
  matrix products  8.23 us (2%)
  other arithmetic  7.95 us (2%)
    all_to_all x2, blocking collectives, moe_layer(): arrived = lax.all_to_all(send, ALL, split_axis=0, concat_axis=0, tiled=True)  188 us
    psum x2, waiting for transfers between devices, moe_layer(): both = lax.psum(jnp.stack([gate_part, up_part]), 'dp')  78.5 us
    all_to_all x2, waiting for transfers between devices, moe_layer(): lax.all_to_all(out.reshape(sources, capacity, piece), ALL, split_axis=0,...  36 us
    all_gather x2, blocking collectives, moe_layer(): hidden_all = lax.all_gather(hidden, 'q', axis=1, tiled=True)  34.2 us
    all_to_all x2, starting transfers between devices, moe_layer(): lax.all_to_all(out.reshape(sources, capacity, piece), ALL, split_axis=0,...  19 us
  transfers between devices with their start and end apart: 6, of which 5 were waited for; matrix products, arithmetic and copies ran while one was open for 2% of the time, Pallas kernels for 0%

commit v1 on v0

--- a/solution.py
+++ b/solution.py
@@ -56,7 +56,7 @@
     rows = arrived.reshape(sources * capacity, half)
     gate_part = jnp.dot(rows, gate_w, preferred_element_type=jnp.float32)
     up_part = jnp.dot(rows, up_w, preferred_element_type=jnp.float32)
-    both = lax.psum(jnp.stack([gate_part, up_part]), "dp")
+    both = jnp.sum(lax.all_gather(jnp.stack([gate_part, up_part]), "dp"), axis=0)
     hidden = (jax.nn.silu(both[0]) * both[1]).astype(jnp.bfloat16)
     hidden_all = lax.all_gather(hidden, "q", axis=1, tiled=True)
     out = lax.dot_general(

time: 415 us -> 337 us (0.81)
  waiting for transfers between devices: 119 us -> 41 us
  blocking collectives: 222 us -> 246 us
  between operations: 13.7 us -> 0.35 us
  starting transfers between devices: 28.4 us -> 21 us
    psum x2 -> x0, waiting for transfers between devices: 78.5 us -> none  [moe_layer(): both = lax.psum(jnp.stack([gate_part, up_part]), 'dp')]
    all_gather x0 -> x2, blocking collectives: none -> 21.8 us  [moe_layer(): lax.all_gather(jnp.stack([gate_part, up_part]), 'dp')]
    all_to_all x2, starting transfers between devices: 19 us -> 11.6 us  [moe_layer(): lax.all_to_all(out.reshape(sources, capacity, piece), ALL, split_axis=0,...]
  transfers between devices with their start and end apart: 6 -> 4, of which waited for: 5 -> 3; matrix products, arithmetic and copies ran while one was open for 2% -> 2% of each run, Pallas kernels for 0% -> 0%
where the time goes in v1:
time: 337 us; the launch traced here: 336 us
  blocking collectives  246 us (73%)
  waiting for transfers between devices  41 us (12%)
  starting transfers between devices  21 us (6%)
  local copies, waits for them, and re-layouts  15 us (4%)
  matrix products  8.22 us (2%)
  other arithmetic  4.59 us (1%)
    all_to_all x2, blocking collectives, moe_layer(): arrived = lax.all_to_all(send, ALL, split_axis=0, concat_axis=0, tiled=True)  187 us
    all_gather x2, blocking collectives, moe_layer(): hidden_all = lax.all_gather(hidden, 'q', axis=1, tiled=True)  36.4 us
    all_to_all x2, waiting for transfers between devices, moe_layer(): lax.all_to_all(out.reshape(sources, capacity, piece), ALL, split_axis=0,...  36.1 us
    all_gather x2, blocking collectives, moe_layer(): lax.all_gather(jnp.stack([gate_part, up_part]), 'dp')  21.8 us
    all_to_all x2, starting transfers between devices, moe_layer(): lax.all_to_all(out.reshape(sources, capacity, piece), ALL, split_axis=0,...  11.6 us
  transfers between devices with their start and end apart: 4, of which 3 were waited for; matrix products, arithmetic and copies ran while one was open for 2% of the time, Pallas kernels for 0%

profile of v1, /device:TPU:1, one launch (start us, length us, event | category | flops | bytes accessed | tf_op | source)
XLA Modules:
  0.0 335.9 jit_solution(18280575248118692250)
XLA Ops:
  0.0 0.8 fusion.36
  2.5 1.1 fusion.16
  3.6 1.2 convolution_convert_fusion.1
  5.5 98.3 %all_to_all.25 = bf16[64,5,3584]{2,1,0:T(8,128)(2,1)} all-to-all(bf16[64,5,3584]{2,1,0:T(8,128)(2,1)S(1)} %bitcast.105), channel_id=1, replica_groups=mesh['section'=8,'eg'=4,'q'=8,'dp'=2] {'eg','q','dp'}, dimensions={0} | all-to-all | bytes 4587520 | tf_op jit(solution)/shard_map/all_to_all | solution.py:54
  103.8 6.3 %all-to-all-start.1 = ((bf16[8,448,128]{2,1,0:T(8,128)(2,1)}), bf16[8,448,128]{2,1,0:T(8,128)(2,1)}, u32[]{:S(2)}, u32[]{:S(2)}) async-start(bf16[8,448,128]{2,1,0:T(8,128)(2,1)} %bitcast.15), calls=%async_computation.1 | async-start | bytes 1835008 | tf_op jit(solution)/shard_map/all_to_all | solution.py:84
  110.0 3.2 reshape.111
  113.2 0.8 convolution_bitcast_fusion.2
  115.2 13.8 %all-gather = f32[4,320,128]{2,1,0:T(8,128)S(1)} all-gather(f32[2,320,128]{2,1,0:T(8,128)S(1)} %pad_maximum_fusion), channel_id=2, replica_groups=mesh['section'=8,'eg'=4,'q'=8,'dp'=2] {'dp'}, dimensions={0}, use_global_device_ids=true | all-gather | bytes 983040 | tf_op jit(solution)/shard_map/all_gather | solution.py:59
  129.1 17.0 %all_gather.20 = bf16[320,1024]{1,0:T(8,128)(2,1)S(1)} all-gather(bf16[320,128]{1,0:T(8,128)(2,1)S(1)} %fusion.23), channel_id=1, replica_groups=mesh['section'=8,'eg'=4,'q'=8,'dp'=2] {'q'}, dimensions={1}, use_global_device_ids=true | all-gather | bytes 737280 | tf_op jit(solution)/shard_map/all_gather | solution.py:61
  146.1 1.7 convolution_convert_fusion.3
  147.8 1.0 reshape.113
  148.8 6.0 %all-to-all-start.2 = ((bf16[64,5,448]{2,1,0:T(8,128)(2,1)}), bf16[64,5,448]{2,1,0:T(8,128)(2,1)S(1)}, u32[]{:S(2)}, u32[]{:S(2)}) async-start(bf16[64,5,448]{2,1,0:T(8,128)(2,1)} %reshape.113), calls=%async_computation.2 | async-start | bytes 1048576 | tf_op jit(solution)/shard_map/all_to_all | solution.py:66
  154.9 18.0 %all-to-all-done.2 = bf16[64,5,448]{2,1,0:T(8,128)(2,1)S(1)} async-done(((bf16[64,5,448]{2,1,0:T(8,128)(2,1)}), bf16[64,5,448]{2,1,0:T(8,128)(2,1)S(1)}, u32[]{:S(2)}, u32[]{:S(2)}) %all-to-all-start.2) | async-done | bytes 286752 | tf_op jit(solution)/shard_map/all_to_all | solution.py:66
  175.3 3.2 collective-permute-start
  178.6 5.0 %collective-permute-done = bf16[8,7168]{1,0:T(8,128)(2,1)S(1)} collective-permute-done((bf16[8,7168]{1,0:T(8,128)(2,1)S(1)}, bf16[8,7168]{1,0:T(8,128)(2,1)S(1)}, u32[]{:S(2)}, u32[]{:S(2)}) %collective-permute-start) | collective-permute-done | bytes 114720 | tf_op jit(solution)/shard_map/ppermute | solution.py:14
  184.7 89.1 %all_to_all.26 = bf16[64,5,3584]{2,1,0:T(8,128)(2,1)} all-to-all(bf16[64,5,3584]{2,1,0:T(8,128)(2,1)S(1)} %bitcast.106), channel_id=1, replica_groups=mesh['section'=8,'eg'=4,'q'=8,'dp'=2] {'eg','q','dp'}, dimensions={0} | all-to-all | bytes 4587520 | tf_op jit(solution)/shard_map/all_to_all | solution.py:54
  273.7 3.2 reshape.117
  276.9 0.8 convolution_bitcast_fusion
  278.9 8.0 %all-gather.1 = f32[4,320,128]{2,1,0:T(8,128)S(1)} all-gather(f32[2,320,128]{2,1,0:T(8,128)S(1)} %pad_maximum_fusion.1), channel_id=3, replica_groups=mesh['section'=8,'eg'=4,'q'=8,'dp'=2] {'dp'}, dimensions={0}, use_global_device_ids=true | all-gather | bytes 983040 | tf_op jit(solution)/shard_map/all_gather | solution.py:59
  287.0 19.4 %all_gather.23 = bf16[320,1024]{1,0:T(8,128)(2,1)S(1)} all-gather(bf16[320,128]{1,0:T(8,128)(2,1)S(1)} %fusion.21), channel_id=1, replica_groups=mesh['section'=8,'eg'=4,'q'=8,'dp'=2] {'q'}, dimensions={1}, use_global_device_ids=true | all-gather | bytes 737280 | tf_op jit(solution)/shard_map/all_gather | solution.py:61
  306.4 1.7 convolution_convert_fusion.2
  308.2 1.0 reshape.118
  309.1 5.6 %all-to-all-start.4 = ((bf16[64,5,448]{2,1,0:T(8,128)(2,1)}), bf16[64,5,448]{2,1,0:T(8,128)(2,1)S(1)}, u32[]{:S(2)}, u32[]{:S(2)}) async-start(bf16[64,5,448]{2,1,0:T(8,128)(2,1)} %reshape.118), calls=%async_computation.4 | async-start | bytes 1048576 | tf_op jit(solution)/shard_map/all_to_all | solution.py:66
  314.8 18.0 %all-to-all-done.4 = bf16[64,5,448]{2,1,0:T(8,128)(2,1)S(1)} async-done(((bf16[64,5,448]{2,1,0:T(8,128)(2,1)}), bf16[64,5,448]{2,1,0:T(8,128)(2,1)S(1)}, u32[]{:S(2)}, u32[]{:S(2)}) %all-to-all-start.4) | async-done | bytes 286752 | tf_op jit(solution)/shard_map/all_to_all | solution.py:66
  (67 shorter events, 11.6 us)
Async XLA Ops:
  0.0 113.2 %copy-start = (bf16[1,3584,128]{2,1,0:T(8,128)(2,1)S(1)}, bf16[1,3584,128]{2,1,0:T(8,128)(2,1)}, u32[]{:S(2)}) copy-start(bf16[1,3584,128]{2,1,0:T(8,128)(2,1)} %param.12) | copy-start | bytes 2752516
  103.8 42.4 %all-to-all-start.1 = ((bf16[8,448,128]{2,1,0:T(8,128)(2,1)}), bf16[8,448,128]{2,1,0:T(8,128)(2,1)}, u32[]{:S(2)}, u32[]{:S(2)}) async-start(bf16[8,448,128]{2,1,0:T(8,128)(2,1)} %bitcast.15), calls=%async_computation.1 | async-start | bytes 1835008 | tf_op jit(solution)/shard_map/all_to_all | solution.py:84
  113.2 1.2 copy-start.1
  146.1 8.7 %copy-start.5 = (f32[1,2,8,2]{2,3,1,0:T(2,128)S(1)}, f32[1,2,8,2]{2,3,1,0:T(2,128)}, u32[]{:S(2)}) copy-start(f32[1,2,8,2]{2,3,1,0:T(2,128)} %param.15) | copy-start | bytes 388
  148.8 24.1 %all-to-all-start.2 = ((bf16[64,5,448]{2,1,0:T(8,128)(2,1)}), bf16[64,5,448]{2,1,0:T(8,128)(2,1)S(1)}, u32[]{:S(2)}, u32[]{:S(2)}) async-start(bf16[64,5,448]{2,1,0:T(8,128)(2,1)} %reshape.113), calls=%async_computation.2 | async-start | bytes 1048576 | tf_op jit(solution)/shard_map/all_to_all | solution.py:66
  173.5 1.7 copy-start.3
  173.5 10.2 %copy-start.4 = (f32[1,7168]{1,0:T(1,128)S(1)}, f32[1,7168]{1,0:T(1,128)}, u32[]{:S(2)}) copy-start(f32[1,7168]{1,0:T(1,128)} %param.10) | copy-start | bytes 86020
  175.3 8.2 %collective-permute-start = (bf16[8,7168]{1,0:T(8,128)(2,1)S(1)}, bf16[8,7168]{1,0:T(8,128)(2,1)S(1)}, u32[]{:S(2)}, u32[]{:S(2)}) collective-permute-start(bf16[8,7168]{1,0:T(8,128)(2,1)S(1)} %fusion.19), channel_id=1, source_target_pairs={{0,64},{64,128},{128,192},{192,256},{256,320},{320,384},{384,448},... | collective-permute-start | bytes 344072 | tf_op jit(solution)/shard_map/ppermute | solution.py:14
  276.9 1.2 copy-start.2
  309.1 23.8 %all-to-all-start.4 = ((bf16[64,5,448]{2,1,0:T(8,128)(2,1)}), bf16[64,5,448]{2,1,0:T(8,128)(2,1)S(1)}, u32[]{:S(2)}, u32[]{:S(2)}) async-start(bf16[64,5,448]{2,1,0:T(8,128)(2,1)} %reshape.118), calls=%async_computation.4 | async-start | bytes 1048576 | tf_op jit(solution)/shard_map/all_to_all | solution.py:66
